TPU v7x, 256 devices: a whole 4x4x8 slice. The times are simulated.
256 devices in a mesh: ctx: 64 (over x, y_hi, z), pipe: 4 (over y_lo, core).
Axes of the slice: x: 4, y: 4 (y_hi: 2, y_lo: 2; y = y_hi * 2 + y_lo), z: 8, core: 2. Of those that a mesh axis runs over, the one named last changes fastest.
Arguments:
- inputs: bfloat16 [4, 8192, 4096], P('pipe', 'ctx'), may hold values from -16 to 16
- q_raw: bfloat16 [4, 8192, 2048], P('pipe', 'ctx'), may hold values from -6 to 6
- grad_out: bfloat16 [4, 8192, 2048], P('pipe', 'ctx'), may hold values from -6 to 6
- segments: int32 [4, 8192], P('pipe'), may hold values from 0 to 4, never falling along the last dimension, each value on 1 to 3072 neighbouring positions
- w_key: bfloat16 [4, 4096, 512], P('pipe', 'ctx'), may hold values from -0.09375 to 0.09375
- w_value: bfloat16 [4, 4096, 512], P('pipe', 'ctx'), may hold values from -0.09375 to 0.09375
- q_gain: float32 [4, 128], P('pipe'), may hold values from 0.1 to 1.9
- k_gain: float32 [4, 128], P('pipe'), may hold values from 0.1 to 1.9
Outputs:
- query_grad: bfloat16 [4, 8192, 2048], P('pipe', 'ctx')
- key_weight_grad: float32 [4, 4096, 512], P('pipe', 'ctx')
- value_weight_grad: float32 [4, 4096, 512], P('pipe', 'ctx')
- section_grad: bfloat16 [4, 8192, 4096], P('pipe', 'ctx')
Inputs may be any that keep to these rules, and one draw needn't show every extreme that they name: `segments`: along each section's sequence the document numbers never fall; every document has 1 to 3072 tokens and one has exactly 3072.
All inputs are finite; a program needn't handle non-finite values.
Results may differ from a plain program's by a relative error of at most 0.019.
Values may be sent and summed in bfloat16 or wider, within the bound.
No kernel may reach another device: no remote copies, remote signals or barrier semaphores. Data moves between devices by JAX's collectives and lax.ppermute only.
A program may use at most 128 MiB of HBM per device.

v0:
```python
import jax
import jax.numpy as jnp
from jax import lax
import functools
from jax.sharding import Mesh, NamedSharding, PartitionSpec as P

HEAD = 128
WINDOW = 768
epsilon = 1e-06
theta_base = 1000000.0


def axis_count(axis):
    names = axis if isinstance(axis, tuple) else (axis,)
    count = 1
    for name in names:
        count *= lax.axis_size(name)
    return count


def passed_along(block, axis, distance):
    devices = range(axis_count(axis))
    route = [(i - distance, i) for i in devices if i - distance in devices]
    return lax.ppermute(block, axis, route)


def shifted(shard, axis, by):
    devices = axis_count(axis)
    return lax.ppermute(shard, axis, [(i, (i + by) % devices) for i in range(devices)])


def rope_tables(positions):
    half_width = HEAD // 2
    frequency = jnp.exp(
        jnp.arange(half_width, dtype=jnp.float32) * (-2.0 * jnp.log(jnp.float32(theta_base)) / HEAD)
    )
    angles = positions.astype(jnp.float32)[:, None] * frequency[None, :]
    return (jnp.cos(angles), jnp.sin(angles))


def rotate(values, cosine, sine_table):
    half_width = values.shape[-1] // 2
    front_half = values[..., :half_width]
    back_half = values[..., half_width:]
    cos_b = cosine[:, None, :]
    sin_b = sine_table[:, None, :]
    return jnp.concatenate(
        [front_half * cos_b - back_half * sin_b, back_half * cos_b + front_half * sin_b], -1
    )


def unrotate(upstream, cosine, sine_table):
    half_width = upstream.shape[-1] // 2
    front_half = upstream[..., :half_width]
    back_half = upstream[..., half_width:]
    cos_b = cosine[:, None, :]
    sin_b = sine_table[:, None, :]
    return jnp.concatenate(
        [front_half * cos_b + back_half * sin_b, back_half * cos_b - front_half * sin_b], -1
    )


def normalize(values, gain_row):
    inverse = lax.rsqrt(jnp.mean(values * values, -1, keepdims=True) + epsilon)
    return (values * inverse * gain_row, inverse)


def normalize_back(values, inverse, gain_row, upstream):
    scaled = upstream * gain_row
    cubed = inverse * inverse * inverse
    return inverse * scaled - values * cubed * jnp.mean(values * scaled, -1, keepdims=True)


def guarded(tile_work, operands):
    return tile_work(*operands)


def local(inputs, q_raw, grad_out, segments, w_key, w_value, q_gain, k_gain, row_parts, col_parts):
    tokens_here = inputs[0]
    tok_rows = tokens_here.shape[0]
    kv_width = w_key.shape[2]
    kv_heads = kv_width // HEAD
    q_heads = q_raw.shape[2] // HEAD
    group = q_heads // kv_heads
    score_scale = HEAD ** (-0.5)
    reach_blocks = WINDOW // tok_rows
    col_index = lax.axis_index("cz")
    ctx_index = lax.axis_index("cb") * col_parts + col_index
    both_rows = jnp.concatenate([w_key[0], w_value[0]], 1)
    weight_slice = lax.all_gather(both_rows, "cz", axis=0, tiled=True)
    inputs_slice = lax.all_to_all(tokens_here, "cb", 1, 0, tiled=True)
    projected = lax.psum_scatter(
        jnp.dot(inputs_slice, weight_slice, preferred_element_type=jnp.float32),
        "cb",
        scatter_dimension=0,
        tiled=True,
    )
    key_raw = projected[:, :kv_width].astype(jnp.bfloat16)
    value_own = projected[:, kv_width:].astype(jnp.bfloat16).reshape(tok_rows, kv_heads, HEAD)
    local_pos = jnp.arange(tok_rows, dtype=jnp.int32)
    positions = ctx_index * tok_rows + local_pos
    cosine, sine_table = rope_tables(positions)
    query_in = q_raw[0].astype(jnp.float32).reshape(tok_rows, q_heads, HEAD)
    query_norm, query_inv = normalize(query_in, q_gain[0])
    query_rot = rotate(query_norm, cosine, sine_table).astype(jnp.bfloat16)
    key_in = key_raw.astype(jnp.float32).reshape(tok_rows, kv_heads, HEAD)
    key_norm, key_inv = normalize(key_in, k_gain[0])
    key_rot = rotate(key_norm, cosine, sine_table).astype(jnp.bfloat16)
    own_pair = jnp.stack([key_rot, value_own])
    key_blocks = [own_pair]
    for distance in range(1, reach_blocks + 1):
        key_blocks.append(passed_along(own_pair, CTX, distance))
    seg_all = segments[0]
    seg_query = lax.dynamic_slice_in_dim(seg_all, ctx_index * tok_rows, tok_rows)
    allowed_list = []
    for distance in range(reach_blocks + 1):
        key_pos = (ctx_index - distance) * tok_rows + local_pos
        seg_key = lax.dynamic_slice_in_dim(
            seg_all, jnp.maximum(ctx_index - distance, 0) * tok_rows, tok_rows
        )
        offset = positions[:, None] - key_pos[None, :]
        allowed = (
            (offset >= 0)
            & (offset < WINDOW)
            & (key_pos >= 0)[None, :]
            & (seg_query[:, None] == seg_key[None, :])
        )
        allowed_list.append(allowed)
    q_group = query_rot.reshape(tok_rows, kv_heads, group, HEAD)
    out_grad = grad_out[0].reshape(tok_rows, kv_heads, group, HEAD)

    def exp_block(key_pair, allowed):
        scores = (
            jnp.einsum("qgrd,kgd->grqk", q_group, key_pair[0], preferred_element_type=jnp.float32)
            * score_scale
        )
        return jnp.where(allowed, jnp.exp(scores), 0.0)

    def total_block(key_pair, allowed):
        return jnp.sum(exp_block(key_pair, allowed), -1)

    zero_total = jnp.zeros((kv_heads, group, tok_rows), jnp.float32)
    row_total = zero_total
    for distance in range(reach_blocks + 1):
        row_total = row_total + guarded(total_block, (key_blocks[distance], allowed_list[distance]))

    def prob_block(key_pair, allowed):
        prob_tile = (exp_block(key_pair, allowed) / row_total[..., None]).astype(jnp.bfloat16)
        out_tile = jnp.einsum(
            "grqk,kgd->qgrd", prob_tile, key_pair[1], preferred_element_type=jnp.float32
        )
        return (prob_tile, out_tile)

    zero_query = jnp.zeros((tok_rows, kv_heads, group, HEAD), jnp.float32)
    prob_list = []
    attn_out = zero_query
    for distance in range(reach_blocks + 1):
        prob_tile, out_tile = guarded(prob_block, (key_blocks[distance], allowed_list[distance]))
        prob_list.append(prob_tile)
        attn_out = attn_out + out_tile
    row_delta = jnp.sum(out_grad.astype(jnp.float32) * attn_out, -1).transpose(1, 2, 0)[..., None]

    def grad_block(key_pair, prob_tile):
        prob_grad = jnp.einsum(
            "qgrd,kgd->grqk", out_grad, key_pair[1], preferred_element_type=jnp.float32
        )
        score_grad = (prob_tile.astype(jnp.float32) * (prob_grad - row_delta)).astype(jnp.bfloat16)
        value_grad = jnp.einsum(
            "grqk,qgrd->kgd", prob_tile, out_grad, preferred_element_type=jnp.float32
        )
        key_grad = (
            jnp.einsum("grqk,qgrd->kgd", score_grad, q_group, preferred_element_type=jnp.float32)
            * score_scale
        )
        query_part = (
            jnp.einsum(
                "grqk,kgd->qgrd", score_grad, key_pair[0], preferred_element_type=jnp.float32
            )
            * score_scale
        )
        return (query_part, jnp.stack([key_grad, value_grad]))

    zero_pair = jnp.zeros((2, tok_rows, kv_heads, HEAD), jnp.float32)
    query_rot_grad = zero_query
    kv_total = zero_pair
    for distance in range(reach_blocks + 1):
        query_part, kv_part = guarded(grad_block, (key_blocks[distance], prob_list[distance]))
        query_rot_grad = query_rot_grad + query_part
        if distance == 0:
            kv_total = kv_part
        else:
            returned = passed_along(kv_part.astype(jnp.bfloat16), CTX, -distance)
            kv_total = kv_total + returned.astype(jnp.float32)
    query_grad = normalize_back(
        query_in,
        query_inv,
        q_gain[0],
        unrotate(query_rot_grad.reshape(tok_rows, q_heads, HEAD), cosine, sine_table),
    )
    query_grad = query_grad.reshape(tok_rows, q_heads * HEAD).astype(jnp.bfloat16)
    key_back = normalize_back(key_in, key_inv, k_gain[0], unrotate(kv_total[0], cosine, sine_table))
    key_back = key_back.reshape(tok_rows, kv_width).astype(jnp.bfloat16)
    value_back = kv_total[1].reshape(tok_rows, kv_width).astype(jnp.bfloat16)
    both_back = jnp.concatenate([key_back, value_back], 1)
    group_back = lax.all_gather(both_back, "cb", axis=0, tiled=True)
    grad_rows = lax.psum_scatter(
        lax.dot_general(
            inputs_slice, group_back, (((0,), (0,)), ((), ())), preferred_element_type=jnp.float32
        ),
        "cz",
        scatter_dimension=0,
        tiled=True,
    )
    slice_grad = lax.dot_general(
        group_back, weight_slice, (((1,), (1,)), ((), ())), preferred_element_type=jnp.float32
    ).astype(jnp.bfloat16)
    input_grad = lax.all_to_all(slice_grad, "cb", 0, 1, tiled=True)
    passed = shifted(input_grad, "pipe", -1)
    return (
        query_grad[None],
        grad_rows[:, :kv_width][None],
        grad_rows[:, kv_width:][None],
        passed[None],
    )


CTX = ("cb", "cz")


def solution(mesh):
    col_parts = 8
    row_parts = mesh.shape["ctx"] // col_parts
    grid = mesh.devices.reshape(row_parts, col_parts, mesh.shape["pipe"])
    split_mesh = Mesh(grid, ("cb", "cz", "pipe"))
    rows = P("pipe", CTX, None)
    inner = jax.shard_map(
        functools.partial(local, row_parts=row_parts, col_parts=col_parts),
        mesh=split_mesh,
        in_specs=(rows, rows, rows, P("pipe", None), rows, rows, P("pipe", None), P("pipe", None)),
        out_specs=(rows, rows, rows, rows),
        check_vma=False,
    )
    placed = NamedSharding(mesh, P("pipe", "ctx", None))

    def run(*args):
        return tuple((lax.with_sharding_constraint(out, placed) for out in inner(*args)))

    return run
```

profile of v0, /device:TPU:1, one launch (start us, length us, event | category | flops | bytes accessed | tf_op | source)
XLA Modules:
  0.0 400.0 jit_solution(7884223318868163470)
XLA Ops:
  7.2 1.5 pad_maximum_fusion.11
  8.8 1.6 copy.260
  10.4 22.6 %all_to_all.38 = bf16[128,8,512]{0,2,1:T(8,128)(2,1)S(1)} all-to-all(bf16[128,8,512]{0,2,1:T(8,128)(2,1)S(1)} %bitcast.575), channel_id=1, replica_groups=mesh['cb'=8,'cz'=8,'pipe'=4] {'cb'}, dimensions={1} | all-to-all | bytes 2097152 | tf_op jit(solution)/shard_map/all_to_all | solution.py:91
  33.6 14.6 %all-gather.3.cloned.1.call-done = bf16[512,1024]{1,0:T(8,128)(2,1)} async-done(((bf16[64,1024]{1,0:T(8,128)(2,1)}), bf16[512,1024]{1,0:T(8,128)(2,1)}) %all-gather.3.cloned.1.call-update) | async-done | bytes 1048592 | tf_op jit(solution)/shard_map/all_gather | solution.py:90
  48.2 4.5 %convolution_bitcast_fusion = f32[1024,1024]{0,1:T(8,128)} fusion(bf16[512,1024]{1,0:T(8,128)(2,1)} %all-gather.3.cloned.1.call-done, bf16[1024,512]{1,0:T(8,128)(2,1)S(1)} %bitcast.586), kind=kOutput, calls=%fused_computation | convolution fusion | flops 1073741824 | bytes 6291456 | tf_op jit(solution)/shard_map/dot_general | solution.py:93
  57.0 1.3 copy.266
  61.5 83.1 %reduce-scatter.5.cloned.1.call-done = f32[128,1024]{0,1:T(8,128)} async-done(((f32[1024,1024]{0,1:T(8,128)}), f32[128,1024]{0,1:T(8,128)}) %reduce-scatter.5.cloned.1.call-update) | async-done | bytes 524304 | tf_op jit(solution)/shard_map/reduce_scatter | solution.py:92
  147.6 3.2 collective-permute-start
  150.8 6.4 %collective-permute-start.2 = (bf16[2,128,4,128]{3,1,2,0:T(8,128)(2,1)S(1)}, bf16[2,128,4,128]{3,1,2,0:T(8,128)(2,1)S(1)}, u32[]{:S(2)}, u32[]{:S(2)}) collective-permute-start(bf16[2,128,4,128]{3,1,2,0:T(8,128)(2,1)S(1)} %pad_maximum_fusion.2), channel_id=1, source_target_pairs={{0,12},{4,16},{8,20},{12,24},{16,28},{20,32},{24,36},{28,40},{32,4... | collective-permute-start | bytes 786440 | tf_op jit(solution)/shard_map/ppermute | solution.py:24
  157.2 2.2 collective-permute-start.3
  159.4 6.2 %collective-permute-start.4 = (bf16[2,128,4,128]{3,1,2,0:T(8,128)(2,1)S(1)}, bf16[2,128,4,128]{3,1,2,0:T(8,128)(2,1)S(1)}, u32[]{:S(2)}, u32[]{:S(2)}) collective-permute-start(bf16[2,128,4,128]{3,1,2,0:T(8,128)(2,1)S(1)} %pad_maximum_fusion.2), channel_id=1, source_target_pairs={{0,20},{4,24},{8,28},{12,32},{16,36},{20,40},{24,44},{28,48},{32,5... | collective-permute-start | bytes 786440 | tf_op jit(solution)/shard_map/ppermute | solution.py:24
  165.6 6.1 %collective-permute-start.5 = (bf16[2,128,4,128]{3,1,2,0:T(8,128)(2,1)S(1)}, bf16[2,128,4,128]{3,1,2,0:T(8,128)(2,1)S(1)}, u32[]{:S(2)}, u32[]{:S(2)}) collective-permute-start(bf16[2,128,4,128]{3,1,2,0:T(8,128)(2,1)S(1)} %pad_maximum_fusion.2), channel_id=1, source_target_pairs={{0,24},{4,28},{8,32},{12,36},{16,40},{20,44},{24,48},{28,52},{32,5... | collective-permute-start | bytes 786440 | tf_op jit(solution)/shard_map/ppermute | solution.py:24
  172.2 3.4 collective-permute-start.1
  177.9 8.5 %collective-permute-done.4 = bf16[2,128,4,128]{3,1,2,0:T(8,128)(2,1)S(1)} collective-permute-done((bf16[2,128,4,128]{3,1,2,0:T(8,128)(2,1)S(1)}, bf16[2,128,4,128]{3,1,2,0:T(8,128)(2,1)S(1)}, u32[]{:S(2)}, u32[]{:S(2)}) %collective-permute-start.4) | collective-permute-done | bytes 262176 | tf_op jit(solution)/shard_map/ppermute | solution.py:24
  186.9 12.1 %collective-permute-done.5 = bf16[2,128,4,128]{3,1,2,0:T(8,128)(2,1)S(1)} collective-permute-done((bf16[2,128,4,128]{3,1,2,0:T(8,128)(2,1)S(1)}, bf16[2,128,4,128]{3,1,2,0:T(8,128)(2,1)S(1)}, u32[]{:S(2)}, u32[]{:S(2)}) %collective-permute-start.5) | collective-permute-done | bytes 262176 | tf_op jit(solution)/shard_map/ppermute | solution.py:24
  206.0 1.3 collective-permute-start.6
  208.0 1.3 collective-permute-start.7
  209.9 1.3 collective-permute-start.8
  211.9 1.3 collective-permute-start.9
  213.8 1.4 collective-permute-start.10
  216.8 1.3 collective-permute-start.11
  218.7 9.8 %collective-permute-done.7 = bf16[2,128,4,128]{3,1,2,0:T(8,128)(2,1)S(1)} collective-permute-done((bf16[2,128,4,128]{3,1,2,0:T(8,128)(2,1)S(1)}, bf16[2,128,4,128]{3,1,2,0:T(8,128)(2,1)S(1)}, u32[]{:S(2)}, u32[]{:S(2)}) %collective-permute-start.7) | collective-permute-done | bytes 262176 | tf_op jit(solution)/shard_map/ppermute | solution.py:24
  228.5 9.2 %collective-permute-done.8 = bf16[2,128,4,128]{3,1,2,0:T(8,128)(2,1)S(1)} collective-permute-done((bf16[2,128,4,128]{3,1,2,0:T(8,128)(2,1)S(1)}, bf16[2,128,4,128]{3,1,2,0:T(8,128)(2,1)S(1)}, u32[]{:S(2)}, u32[]{:S(2)}) %collective-permute-start.8) | collective-permute-done | bytes 262176 | tf_op jit(solution)/shard_map/ppermute | solution.py:24
  237.8 13.4 %collective-permute-done.11 = bf16[2,128,4,128]{3,1,2,0:T(8,128)(2,1)S(1)} collective-permute-done((bf16[2,128,4,128]{3,1,2,0:T(8,128)(2,1)S(1)}, bf16[2,128,4,128]{3,1,2,0:T(8,128)(2,1)S(1)}, u32[]{:S(2)}, u32[]{:S(2)}) %collective-permute-start.11) | collective-permute-done | bytes 262176 | tf_op jit(solution)/shard_map/ppermute | solution.py:24
  255.0 1.2 mul.517
  256.2 1.2 mul.518
  257.4 1.2 mul.597
  259.7 74.3 %all-gather.5.cloned.1.call-done = bf16[1024,1024]{0,1:T(8,128)(2,1)} async-done(((bf16[128,1024]{0,1:T(8,128)(2,1)}), bf16[1024,1024]{0,1:T(8,128)(2,1)}) %all-gather.5.cloned.1.call-update) | async-done | bytes 2097168 | tf_op jit(solution)/shard_map/all_gather | solution.py:205
  333.9 4.5 %convolution_bitcast_fusion.1 = f32[512,1024]{0,1:T(8,128)} fusion(bf16[1024,1024]{0,1:T(8,128)(2,1)} %all-gather.5.cloned.1.call-done, bf16[1024,512]{1,0:T(8,128)(2,1)} %bitcast.587), kind=kOutput, calls=%fused_computation.1 | convolution fusion | flops 1073741824 | bytes 5242880 | tf_op jit(solution)/shard_map/dot_general | solution.py:207
  338.4 2.9 copy.460
  342.7 2.3 fusion.97
  345.0 1.4 fusion.98
  346.4 1.3 fusion.99
  347.7 1.3 fusion.100
  349.0 1.4 convolution_add_fusion.1
  350.4 2.3 convolution_convert_fusion
  352.7 3.7 all-to-all-start.1
  356.5 3.0 fusion.12
  360.5 1.6 copy.462
  362.1 2.4 copy.463
  364.5 2.8 multiply_add_fusion
  367.3 3.4 all-to-all-done.1
  371.9 2.8 collective-permute-start.12
  375.3 1.3 mul.602
  376.6 2.5 mul.603
  380.3 2.9 fusion.88
  383.2 5.1 %collective-permute-done.12 = bf16[128,4096]{1,0:T(8,128)(2,1)} collective-permute-done((bf16[128,4096]{1,0:T(8,128)(2,1)}, bf16[128,4096]{1,0:T(8,128)(2,1)}, u32[]{:S(2)}, u32[]{:S(2)}) %collective-permute-start.12) | collective-permute-done | bytes 1048608 | tf_op jit(solution)/shard_map/ppermute | solution.py:29
  391.1 2.3 copy.472
  (230 shorter events, 38.1 us)
Async XLA Ops:
  7.2 41.1 %all-gather.3.cloned.1.call-start = ((), (), s32[]{:S(2)}) async-start(), calls=%async_computation.4 | async-start | bytes 1179648 | tf_op jit(solution)/shard_map/all_gather | solution.py:90
  8.8 135.9 %reduce-scatter.5.cloned.1.call-start = ((), (), s32[]{:S(2)}) async-start(), calls=%async_computation.5 | async-start | bytes 4718592 | tf_op jit(solution)/shard_map/reduce_scatter | solution.py:92
  33.6 19.2 %copy-start.29 = (bf16[8,128,512]{2,1,0:T(8,128)(2,1)}, bf16[8,128,512]{2,1,0:T(8,128)(2,1)S(1)}, u32[]{:S(2)}) copy-start(bf16[8,128,512]{2,1,0:T(8,128)(2,1)S(1)} %copy.261) | copy-start | bytes 3145732
  52.8 281.1 %all-gather.5.cloned.1.call-start = ((), (), s32[]{:S(2)}) async-start(), calls=%async_computation.6 | async-start | bytes 2359296 | tf_op jit(solution)/shard_map/all_gather | solution.py:205
  59.7 87.5 %copy-start.20 = (f32[128,64]{1,0:T(8,128)S(1)}, f32[128,64]{1,0:T(8,128)}, u32[]{:S(2)}) copy-start(f32[128,64]{1,0:T(8,128)} %copy-done.19) | copy-start | bytes 98308
  59.7 87.5 %copy-start.24 = (f32[128,64]{1,0:T(8,128)S(1)}, f32[128,64]{1,0:T(8,128)}, u32[]{:S(2)}) copy-start(f32[128,64]{1,0:T(8,128)} %copy-done.23) | copy-start | bytes 98308
  145.8 56.8 %copy-start.17 = (bf16[128,512]{0,1:T(8,128)(2,1)}, bf16[128,512]{0,1:T(8,128)(2,1)S(1)}, u32[]{:S(2)}) copy-start(bf16[128,512]{0,1:T(8,128)(2,1)S(1)} %slice.130) | copy-start | bytes 393220
  146.6 25.1 %copy-start.46 = (pred[128,128]{0,1:T(8,128)(4,1)S(1)}, pred[128,128]{0,1:T(8,128)(4,1)}, u32[]{:S(2)}) copy-start(pred[128,128]{0,1:T(8,128)(4,1)} %get-tuple-element.62) | copy-start | bytes 49156
  147.3 29.4 %copy-start.14 = (bf16[128,4,64]{2,0,1:T(8,128)(2,1)}, bf16[128,4,64]{2,0,1:T(8,128)(2,1)S(1)}, u32[]{:S(2)}) copy-start(bf16[128,4,64]{2,0,1:T(8,128)(2,1)S(1)} %get-tuple-element.35) | copy-start | bytes 196612
  147.5 29.2 %copy-start.45 = (pred[128,128]{0,1:T(8,128)(4,1)S(1)}, pred[128,128]{0,1:T(8,128)(4,1)}, u32[]{:S(2)}) copy-start(pred[128,128]{0,1:T(8,128)(4,1)} %get-tuple-element.59) | copy-start | bytes 49156
  147.6 24.5 %collective-permute-start = (bf16[2,128,4,128]{3,1,2,0:T(8,128)(2,1)S(1)}, bf16[2,128,4,128]{3,1,2,0:T(8,128)(2,1)S(1)}, u32[]{:S(2)}, u32[]{:S(2)}) collective-permute-start(bf16[2,128,4,128]{3,1,2,0:T(8,128)(2,1)S(1)} %pad_maximum_fusion.2), channel_id=1, source_target_pairs={{0,4},{4,8},{8,12},{12,16},{16,20},{20,24},{24,28},{28,32},{32,36}... | collective-permute-start | bytes 786440 | tf_op jit(solution)/shard_map/ppermute | solution.py:24
  150.8 25.9 %collective-permute-start.2 = (bf16[2,128,4,128]{3,1,2,0:T(8,128)(2,1)S(1)}, bf16[2,128,4,128]{3,1,2,0:T(8,128)(2,1)S(1)}, u32[]{:S(2)}, u32[]{:S(2)}) collective-permute-start(bf16[2,128,4,128]{3,1,2,0:T(8,128)(2,1)S(1)} %pad_maximum_fusion.2), channel_id=1, source_target_pairs={{0,12},{4,16},{8,20},{12,24},{16,28},{20,32},{24,36},{28,40},{32,4... | collective-permute-start | bytes 786440 | tf_op jit(solution)/shard_map/ppermute | solution.py:24
  157.2 20.4 %collective-permute-start.3 = (bf16[2,128,4,128]{3,1,2,0:T(8,128)(2,1)S(1)}, bf16[2,128,4,128]{3,1,2,0:T(8,128)(2,1)S(1)}, u32[]{:S(2)}, u32[]{:S(2)}) collective-permute-start(bf16[2,128,4,128]{3,1,2,0:T(8,128)(2,1)S(1)} %pad_maximum_fusion.2), channel_id=1, source_target_pairs={{0,16},{4,20},{8,24},{12,28},{16,32},{20,36},{24,40},{28,44},{32,4... | collective-permute-start | bytes 786440 | tf_op jit(solution)/shard_map/ppermute | solution.py:24
  159.4 27.1 %collective-permute-start.4 = (bf16[2,128,4,128]{3,1,2,0:T(8,128)(2,1)S(1)}, bf16[2,128,4,128]{3,1,2,0:T(8,128)(2,1)S(1)}, u32[]{:S(2)}, u32[]{:S(2)}) collective-permute-start(bf16[2,128,4,128]{3,1,2,0:T(8,128)(2,1)S(1)} %pad_maximum_fusion.2), channel_id=1, source_target_pairs={{0,20},{4,24},{8,28},{12,32},{16,36},{20,40},{24,44},{28,48},{32,5... | collective-permute-start | bytes 786440 | tf_op jit(solution)/shard_map/ppermute | solution.py:24
  165.6 33.4 %collective-permute-start.5 = (bf16[2,128,4,128]{3,1,2,0:T(8,128)(2,1)S(1)}, bf16[2,128,4,128]{3,1,2,0:T(8,128)(2,1)S(1)}, u32[]{:S(2)}, u32[]{:S(2)}) collective-permute-start(bf16[2,128,4,128]{3,1,2,0:T(8,128)(2,1)S(1)} %pad_maximum_fusion.2), channel_id=1, source_target_pairs={{0,24},{4,28},{8,32},{12,36},{16,40},{20,44},{24,48},{28,52},{32,5... | collective-permute-start | bytes 786440 | tf_op jit(solution)/shard_map/ppermute | solution.py:24
  172.1 5.4 %copy-start.44 = (pred[128,128]{0,1:T(8,128)(4,1)S(1)}, pred[128,128]{0,1:T(8,128)(4,1)}, u32[]{:S(2)}) copy-start(pred[128,128]{0,1:T(8,128)(4,1)} %get-tuple-element.60) | copy-start | bytes 49156
  172.1 33.2 %copy-start.39 = (bf16[2,128,4,128]{3,1,2,0:T(8,128)(2,1)}, bf16[2,128,4,128]{3,1,2,0:T(8,128)(2,1)S(1)}, u32[]{:S(2)}) copy-start(bf16[2,128,4,128]{3,1,2,0:T(8,128)(2,1)S(1)} %collective-permute-done) | copy-start | bytes 786436
  172.2 27.2 %collective-permute-start.1 = (bf16[2,128,4,128]{3,1,2,0:T(8,128)(2,1)S(1)}, bf16[2,128,4,128]{3,1,2,0:T(8,128)(2,1)S(1)}, u32[]{:S(2)}, u32[]{:S(2)}) collective-permute-start(bf16[2,128,4,128]{3,1,2,0:T(8,128)(2,1)S(1)} %pad_maximum_fusion.2), channel_id=1, source_target_pairs={{0,8},{4,12},{8,16},{12,20},{16,24},{20,28},{24,32},{28,36},{32,40... | collective-permute-start | bytes 786440 | tf_op jit(solution)/shard_map/ppermute | solution.py:24
  176.7 9.8 %copy-start.43 = (pred[128,128]{0,1:T(8,128)(4,1)S(1)}, pred[128,128]{0,1:T(8,128)(4,1)}, u32[]{:S(2)}) copy-start(pred[128,128]{0,1:T(8,128)(4,1)} %get-tuple-element.61) | copy-start | bytes 49156
  176.7 32.5 %copy-start.32 = (bf16[2,128,4,128]{3,1,2,0:T(8,128)(2,1)}, bf16[2,128,4,128]{3,1,2,0:T(8,128)(2,1)S(1)}, u32[]{:S(2)}) copy-start(bf16[2,128,4,128]{3,1,2,0:T(8,128)(2,1)S(1)} %collective-permute-done.2) | copy-start | bytes 786436
  177.5 33.7 %copy-start.33 = (bf16[2,128,4,128]{3,1,2,0:T(8,128)(2,1)}, bf16[2,128,4,128]{3,1,2,0:T(8,128)(2,1)S(1)}, u32[]{:S(2)}) copy-start(bf16[2,128,4,128]{3,1,2,0:T(8,128)(2,1)S(1)} %collective-permute-done.3) | copy-start | bytes 786436
  177.9 21.5 %copy-start.42 = (pred[128,128]{0,1:T(8,128)(4,1)S(1)}, pred[128,128]{0,1:T(8,128)(4,1)}, u32[]{:S(2)}) copy-start(pred[128,128]{0,1:T(8,128)(4,1)} %get-tuple-element.58) | copy-start | bytes 49156
  186.5 26.7 %copy-start.35 = (bf16[2,128,4,128]{3,1,2,0:T(8,128)(2,1)}, bf16[2,128,4,128]{3,1,2,0:T(8,128)(2,1)S(1)}, u32[]{:S(2)}) copy-start(bf16[2,128,4,128]{3,1,2,0:T(8,128)(2,1)S(1)} %collective-permute-done.4) | copy-start | bytes 786436
  199.0 16.3 %copy-start.37 = (bf16[2,128,4,128]{3,1,2,0:T(8,128)(2,1)}, bf16[2,128,4,128]{3,1,2,0:T(8,128)(2,1)S(1)}, u32[]{:S(2)}) copy-start(bf16[2,128,4,128]{3,1,2,0:T(8,128)(2,1)S(1)} %collective-permute-done.5) | copy-start | bytes 786436
  199.4 7.9 %copy-start.30 = (bf16[2,128,4,128]{3,1,2,0:T(8,128)(2,1)}, bf16[2,128,4,128]{3,1,2,0:T(8,128)(2,1)S(1)}, u32[]{:S(2)}) copy-start(bf16[2,128,4,128]{3,1,2,0:T(8,128)(2,1)S(1)} %collective-permute-done.1) | copy-start | bytes 786436
  206.0 10.8 %collective-permute-start.6 = (bf16[2,128,4,128]{3,1,2,0:T(8,128)(2,1)S(1)}, bf16[2,128,4,128]{3,1,2,0:T(8,128)(2,1)S(1)}, u32[]{:S(2)}, u32[]{:S(2)}) collective-permute-start(bf16[2,128,4,128]{3,1,2,0:T(8,128)(2,1)S(1)} %pad_maximum_fusion.3), channel_id=1, source_target_pairs={{4,0},{8,4},{12,8},{16,12},{20,16},{24,20},{28,24},{32,28},{36,32}... | collective-permute-start | bytes 786440 | tf_op jit(solution)/shard_map/ppermute | solution.py:24
  208.0 20.6 %collective-permute-start.7 = (bf16[2,128,4,128]{3,1,2,0:T(8,128)(2,1)S(1)}, bf16[2,128,4,128]{3,1,2,0:T(8,128)(2,1)S(1)}, u32[]{:S(2)}, u32[]{:S(2)}) collective-permute-start(bf16[2,128,4,128]{3,1,2,0:T(8,128)(2,1)S(1)} %pad_maximum_fusion.4), channel_id=1, source_target_pairs={{8,0},{12,4},{16,8},{20,12},{24,16},{28,20},{32,24},{36,28},{40,32... | collective-permute-start | bytes 786440 | tf_op jit(solution)/shard_map/ppermute | solution.py:24
  209.9 27.9 %collective-permute-start.8 = (bf16[2,128,4,128]{3,1,2,0:T(8,128)(2,1)S(1)}, bf16[2,128,4,128]{3,1,2,0:T(8,128)(2,1)S(1)}, u32[]{:S(2)}, u32[]{:S(2)}) collective-permute-start(bf16[2,128,4,128]{3,1,2,0:T(8,128)(2,1)S(1)} %pad_maximum_fusion.5), channel_id=1, source_target_pairs={{12,0},{16,4},{20,8},{24,12},{28,16},{32,20},{36,24},{40,28},{44,3... | collective-permute-start | bytes 786440 | tf_op jit(solution)/shard_map/ppermute | solution.py:24
  211.9 25.9 %collective-permute-start.9 = (bf16[2,128,4,128]{3,1,2,0:T(8,128)(2,1)S(1)}, bf16[2,128,4,128]{3,1,2,0:T(8,128)(2,1)S(1)}, u32[]{:S(2)}, u32[]{:S(2)}) collective-permute-start(bf16[2,128,4,128]{3,1,2,0:T(8,128)(2,1)S(1)} %pad_maximum_fusion.6), channel_id=1, source_target_pairs={{16,0},{20,4},{24,8},{28,12},{32,16},{36,20},{40,24},{44,28},{48,3... | collective-permute-start | bytes 786440 | tf_op jit(solution)/shard_map/ppermute | solution.py:24
  213.8 23.9 %collective-permute-start.10 = (bf16[2,128,4,128]{3,1,2,0:T(8,128)(2,1)S(1)}, bf16[2,128,4,128]{3,1,2,0:T(8,128)(2,1)S(1)}, u32[]{:S(2)}, u32[]{:S(2)}) collective-permute-start(bf16[2,128,4,128]{3,1,2,0:T(8,128)(2,1)S(1)} %pad_maximum_fusion.7), channel_id=1, source_target_pairs={{20,0},{24,4},{28,8},{32,12},{36,16},{40,20},{44,24},{48,28},{52,3... | collective-permute-start | bytes 786440 | tf_op jit(solution)/shard_map/ppermute | solution.py:24
  216.8 34.4 %collective-permute-start.11 = (bf16[2,128,4,128]{3,1,2,0:T(8,128)(2,1)S(1)}, bf16[2,128,4,128]{3,1,2,0:T(8,128)(2,1)S(1)}, u32[]{:S(2)}, u32[]{:S(2)}) collective-permute-start(bf16[2,128,4,128]{3,1,2,0:T(8,128)(2,1)S(1)} %pad_maximum_fusion.8), channel_id=1, source_target_pairs={{24,0},{28,4},{32,8},{36,12},{40,16},{44,20},{48,24},{52,28},{56,3... | collective-permute-start | bytes 786440 | tf_op jit(solution)/shard_map/ppermute | solution.py:24
  218.4 33.8 %copy-start.21 = (f32[128,64]{1,0:T(8,128)S(1)}, f32[128,64]{1,0:T(8,128)}, u32[]{:S(2)}) copy-start(f32[128,64]{1,0:T(8,128)} %copy-done.19) | copy-start | bytes 98308
  218.4 33.8 %copy-start.25 = (f32[128,64]{1,0:T(8,128)S(1)}, f32[128,64]{1,0:T(8,128)}, u32[]{:S(2)}) copy-start(f32[128,64]{1,0:T(8,128)} %copy-done.23) | copy-start | bytes 98308
  218.7 33.6 %copy-start.52 = (f32[1,128]{1,0:T(1,128)S(1)}, f32[1,128]{1,0:T(1,128)}, u32[]{:S(2)}) copy-start(f32[1,128]{1,0:T(1,128)} %param.15) | copy-start | bytes 1540
  254.7 133.6 %reduce-scatter.7.cloned.1.call-start = ((), (), s32[]{:S(2)}) async-start(), calls=%async_computation.7 | async-start | bytes 2359296
  342.0 3.0 copy-start.34
  342.7 3.7 copy-start.3
  342.7 3.7 copy-start.36
  352.7 3.7 copy-start.9
  352.7 3.7 copy-start.31
  352.7 18.0 %all-to-all-start.1 = ((bf16[8,128,512]{2,1,0:T(8,128)(2,1)}), bf16[8,128,512]{2,1,0:T(8,128)(2,1)S(1)}, u32[]{:S(2)}, u32[]{:S(2)}) async-start(bf16[8,128,512]{2,1,0:T(8,128)(2,1)} %bitcast.588), calls=%async_computation.2 | async-start | bytes 2097152 | tf_op jit(solution)/shard_map/all_to_all | solution.py:217
  360.5 4.0 %copy-start.22 = (f32[128,64]{1,0:T(8,128)S(1)}, f32[128,64]{1,0:T(8,128)}, u32[]{:S(2)}) copy-start(f32[128,64]{1,0:T(8,128)} %copy-done.19) | copy-start | bytes 98308
  360.5 4.0 %copy-start.26 = (f32[128,64]{1,0:T(8,128)S(1)}, f32[128,64]{1,0:T(8,128)}, u32[]{:S(2)}) copy-start(f32[128,64]{1,0:T(8,128)} %copy-done.23) | copy-start | bytes 98308
  370.8 3.9 copy-start.12
  370.8 3.9 copy-start.13
  371.9 16.5 %collective-permute-start.12 = (bf16[128,4096]{1,0:T(8,128)(2,1)}, bf16[128,4096]{1,0:T(8,128)(2,1)}, u32[]{:S(2)}, u32[]{:S(2)}) collective-permute-start(bf16[128,4096]{1,0:T(8,128)(2,1)} %bitcast.231), channel_id=1, source_target_pairs={{0,3},{1,0},{2,1},{3,2},{4,7},{5,4},{6,5},{7,6},{8,11},{9,8},{10,9... | collective-permute-start | bytes 3145736 | tf_op jit(solution)/shard_map/ppermute | solution.py:29
  376.6 3.7 copy-start.10
  376.6 3.7 copy-start.11
  (27 other events, 54.0 us)
Sparse Core Ops, SparseCore 0:
  10.3 37.8 all-gather.2
  52.9 91.6 reduce-scatter.4
  254.8 79.0 all-gather.4
  341.5 38.8 reduce-scatter.6
where the time goes:
time: 401 us; the launch traced here: 400 us
  waiting for transfers between devices  234 us (58%)
  starting transfers between devices  42.2 us (11%)
  matrix products  34.7 us (9%)
  local copies, waits for them, and re-layouts  34.6 us (9%)
  blocking collectives  22.6 us (6%)
  other arithmetic  16.6 us (4%)
  between operations  15 us (4%)
    reduce_scatter x1, waiting for transfers between devices, local(): lax.psum_scatter(jnp.dot(inputs_slice, weight_slice, preferred_element_ty...  83.1 us
    all_gather x1, waiting for transfers between devices, local(): group_back = lax.all_gather(both_back, 'cb', axis=0, tiled=True)  74.3 us
    ppermute x12, waiting for transfers between devices, passed_along(): return lax.ppermute(block, axis, route)  53.6 us
    ppermute x12, starting transfers between devices, passed_along(): return lax.ppermute(block, axis, route)  35.4 us
    all_to_all x1, blocking collectives, local(): inputs_slice = lax.all_to_all(tokens_here, 'cb', 1, 0, tiled=True)  22.6 us
    unnamed x125, local copies, waits for them, and re-layouts  17.4 us
    all_gather x1, waiting for transfers between devices, local(): weight_slice = lax.all_gather(both_rows, 'cz', axis=0, tiled=True)  14.6 us
    dot_general x7, matrix products, grad_block(): jnp.einsum('grqk,kgd->qgrd', score_grad, key_pair[0], preferred_element_t...  11.1 us
  transfers between devices with their start and end apart: 18, of which 11 were waited for; matrix products, arithmetic and copies ran while one was open for 13% of the time, Pallas kernels for 0%

commit v1 on v0

--- a/solution.py
+++ b/solution.py
@@ -88,7 +88,10 @@
     ctx_index = lax.axis_index("cb") * col_parts + col_index
     both_rows = jnp.concatenate([w_key[0], w_value[0]], 1)
     weight_slice = lax.all_gather(both_rows, "cz", axis=0, tiled=True)
-    inputs_slice = lax.all_to_all(tokens_here, "cb", 1, 0, tiled=True)
+    inputs_slice = jnp.concatenate(
+        lax.all_to_all(jnp.stack(jnp.split(tokens_here, lax.axis_size("cb"), axis=1)), "cb", 0, 0),
+        axis=0,
+    )
     projected = lax.psum_scatter(
         jnp.dot(inputs_slice, weight_slice, preferred_element_type=jnp.float32),
         "cb",

time: 401 us -> 407 us (1.015)
  matrix products: 34.7 us -> 47.3 us
  waiting for transfers between devices: 234 us -> 222 us
    ppermute x12, waiting for transfers between devices: 53.6 us -> 47.8 us  [passed_along(): return lax.ppermute(block, axis, route)]
    all_gather x1, waiting for transfers between devices: 14.6 us -> 9.48 us  [local(): weight_slice = lax.all_gather(both_rows, 'cz', axis=0, tiled=True)]
    mul x4 -> x6, local copies, waits for them, and re-layouts: 6.15 us -> 8.73 us  [normalize_back(): values * cubed * jnp.mean(values * scaled, -1, keepdims=True)]
    unnamed x125 -> x98, local copies, waits for them, and re-layouts: 17.4 us -> 16.8 us
  transfers between devices with their start and end apart: 18 -> 18, of which waited for: 11 -> 10; matrix products, arithmetic and copies ran while one was open for 13% -> 16% of each run, Pallas kernels for 0% -> 0%
where the time goes in v1:
time: 407 us; the launch traced here: 405 us
  waiting for transfers between devices  222 us (55%)
  matrix products  47.3 us (12%)
  starting transfers between devices  42.9 us (11%)
  local copies, waits for them, and re-layouts  38.1 us (9%)
  blocking collectives  22.6 us (6%)
  other arithmetic  17.1 us (4%)
  between operations  14.9 us (4%)
    reduce_scatter x1, waiting for transfers between devices, local(): lax.psum_scatter(jnp.dot(inputs_slice, weight_slice, preferred_element_ty...  85.1 us
    all_gather x1, waiting for transfers between devices, local(): group_back = lax.all_gather(both_back, 'cb', axis=0, tiled=True)  71.8 us
    ppermute x12, waiting for transfers between devices, passed_along(): return lax.ppermute(block, axis, route)  47.8 us
    ppermute x12, starting transfers between devices, passed_along(): return lax.ppermute(block, axis, route)  36.1 us
    all_to_all x1, blocking collectives, local(): lax.all_to_all(jnp.stack(jnp.split(tokens_here, lax.axis_size('cb'), axis...  22.6 us
    unnamed x98, local copies, waits for them, and re-layouts  16.8 us
    dot_general x7, matrix products, grad_block(): jnp.einsum('grqk,kgd->qgrd', score_grad, key_pair[0], preferred_element_t...  14 us
    all_gather x1, waiting for transfers between devices, local(): weight_slice = lax.all_gather(both_rows, 'cz', axis=0, tiled=True)  9.48 us
  transfers between devices with their start and end apart: 18, of which 10 were waited for; matrix products, arithmetic and copies ran while one was open for 16% of the time, Pallas kernels for 0%

profile of v1, /device:TPU:1, one launch (start us, length us, event | category | flops | bytes accessed | tf_op | source)
XLA Modules:
  0.0 405.1 jit_solution(5108274174484886151)
XLA Ops:
  7.2 1.5 pad_maximum_fusion.11
  16.2 22.6 %all_to_all.24 = bf16[8,128,512]{2,1,0:T(8,128)(2,1)S(1)} all-to-all(bf16[8,128,512]{2,1,0:T(8,128)(2,1)S(1)} %fusion.98), channel_id=1, replica_groups=mesh['cb'=8,'cz'=8,'pipe'=4] {'cb'}, dimensions={0} | all-to-all | bytes 2097152 | tf_op jit(solution)/shard_map/all_to_all | solution.py:92
  38.8 9.5 %all-gather.3.cloned.1.call-done = bf16[512,1024]{1,0:T(8,128)(2,1)} async-done(((bf16[64,1024]{1,0:T(8,128)(2,1)}), bf16[512,1024]{1,0:T(8,128)(2,1)}) %all-gather.3.cloned.1.call-update) | async-done | bytes 1048592 | tf_op jit(solution)/shard_map/all_gather | solution.py:90
  48.3 4.5 %fusion.157 = f32[1024,1024]{1,0:T(8,128)} fusion(bf16[1024,512]{1,0:T(8,128)(2,1)S(1)} %bitcast.610, bf16[512,1024]{1,0:T(8,128)(2,1)} %all-gather.3.cloned.1.call-done), kind=kOutput, calls=%fused_computation.305 | convolution fusion | flops 1073741824 | bytes 6291456 | tf_op jit(solution)/shard_map/dot_general | solution.py:96
  59.3 85.1 %reduce-scatter.3.cloned.1.call-done = f32[128,1024]{1,0:T(8,128)} async-done(((f32[1024,1024]{1,0:T(8,128)}), f32[128,1024]{1,0:T(8,128)}) %reduce-scatter.3.cloned.1.call-update) | async-done | bytes 524304 | tf_op jit(solution)/shard_map/reduce_scatter | solution.py:95
  148.9 3.9 collective-permute-start
  152.8 5.7 %collective-permute-start.2 = (bf16[2,128,4,128]{3,1,2,0:T(8,128)(2,1)}, bf16[2,128,4,128]{3,1,2,0:T(8,128)(2,1)S(1)}, u32[]{:S(2)}, u32[]{:S(2)}) collective-permute-start(bf16[2,128,4,128]{3,1,2,0:T(8,128)(2,1)} %pad_maximum_fusion.2), channel_id=1, source_target_pairs={{0,12},{4,16},{8,20},{12,24},{16,28},{20,32},{24,36},{28,40},{32,4... | collective-permute-start | bytes 786440 | tf_op jit(solution)/shard_map/ppermute | solution.py:24
  158.5 2.9 collective-permute-start.3
  161.3 6.2 %collective-permute-start.4 = (bf16[2,128,4,128]{3,1,2,0:T(8,128)(2,1)}, bf16[2,128,4,128]{3,1,2,0:T(8,128)(2,1)}, u32[]{:S(2)}, u32[]{:S(2)}) collective-permute-start(bf16[2,128,4,128]{3,1,2,0:T(8,128)(2,1)} %pad_maximum_fusion.2), channel_id=1, source_target_pairs={{0,20},{4,24},{8,28},{12,32},{16,36},{20,40},{24,44},{28,48},{32,5... | collective-permute-start | bytes 786440 | tf_op jit(solution)/shard_map/ppermute | solution.py:24
  167.5 6.1 %collective-permute-start.5 = (bf16[2,128,4,128]{3,1,2,0:T(8,128)(2,1)}, bf16[2,128,4,128]{3,1,2,0:T(8,128)(2,1)}, u32[]{:S(2)}, u32[]{:S(2)}) collective-permute-start(bf16[2,128,4,128]{3,1,2,0:T(8,128)(2,1)} %pad_maximum_fusion.2), channel_id=1, source_target_pairs={{0,24},{4,28},{8,32},{12,36},{16,40},{20,44},{24,48},{28,52},{32,5... | collective-permute-start | bytes 786440 | tf_op jit(solution)/shard_map/ppermute | solution.py:24
  175.7 3.5 collective-permute-start.1
  179.2 1.3 fusion.156
  180.9 1.3 fusion.152
  182.2 5.5 %collective-permute-done.4 = bf16[2,128,4,128]{3,1,2,0:T(8,128)(2,1)} collective-permute-done((bf16[2,128,4,128]{3,1,2,0:T(8,128)(2,1)}, bf16[2,128,4,128]{3,1,2,0:T(8,128)(2,1)}, u32[]{:S(2)}, u32[]{:S(2)}) %collective-permute-start.4) | collective-permute-done | bytes 262176 | tf_op jit(solution)/shard_map/ppermute | solution.py:24
  189.0 11.5 %collective-permute-done.5 = bf16[2,128,4,128]{3,1,2,0:T(8,128)(2,1)} collective-permute-done((bf16[2,128,4,128]{3,1,2,0:T(8,128)(2,1)}, bf16[2,128,4,128]{3,1,2,0:T(8,128)(2,1)}, u32[]{:S(2)}, u32[]{:S(2)}) %collective-permute-start.5) | collective-permute-done | bytes 262176 | tf_op jit(solution)/shard_map/ppermute | solution.py:24
  200.5 1.3 fusion.150
  212.9 1.3 collective-permute-start.6
  214.9 1.3 collective-permute-start.7
  216.8 1.3 collective-permute-start.8
  219.7 1.3 collective-permute-start.9
  222.6 1.4 collective-permute-start.10
  226.4 1.3 collective-permute-start.11
  228.3 7.1 %collective-permute-done.7 = bf16[2,128,4,128]{3,1,2,0:T(8,128)(2,1)S(1)} collective-permute-done((bf16[2,128,4,128]{3,1,2,0:T(8,128)(2,1)S(1)}, bf16[2,128,4,128]{3,1,2,0:T(8,128)(2,1)S(1)}, u32[]{:S(2)}, u32[]{:S(2)}) %collective-permute-start.7) | collective-permute-done | bytes 262176 | tf_op jit(solution)/shard_map/ppermute | solution.py:24
  235.4 9.3 %collective-permute-done.8 = bf16[2,128,4,128]{3,1,2,0:T(8,128)(2,1)S(1)} collective-permute-done((bf16[2,128,4,128]{3,1,2,0:T(8,128)(2,1)S(1)}, bf16[2,128,4,128]{3,1,2,0:T(8,128)(2,1)S(1)}, u32[]{:S(2)}, u32[]{:S(2)}) %collective-permute-start.8) | collective-permute-done | bytes 262176 | tf_op jit(solution)/shard_map/ppermute | solution.py:24
  244.6 14.4 %collective-permute-done.11 = bf16[2,128,4,128]{3,1,2,0:T(8,128)(2,1)S(1)} collective-permute-done((bf16[2,128,4,128]{3,1,2,0:T(8,128)(2,1)S(1)}, bf16[2,128,4,128]{3,1,2,0:T(8,128)(2,1)S(1)}, u32[]{:S(2)}, u32[]{:S(2)}) %collective-permute-start.11) | collective-permute-done | bytes 262176 | tf_op jit(solution)/shard_map/ppermute | solution.py:24
  265.8 1.3 mul.597
  267.1 2.3 mul.598
  269.4 71.8 %all-gather.5.cloned.1.call-done = bf16[1024,1024]{1,0:T(8,128)(2,1)} async-done(((bf16[128,1024]{1,0:T(8,128)(2,1)}), bf16[1024,1024]{1,0:T(8,128)(2,1)}) %all-gather.5.cloned.1.call-update) | async-done | bytes 2097168 | tf_op jit(solution)/shard_map/all_gather | solution.py:208
  341.3 4.2 %fusion.159 = f32[512,1024]{1,0:T(8,128)} fusion(bf16[1024,512]{1,0:T(8,128)(2,1)S(1)} %bitcast.611, bf16[1024,1024]{1,0:T(8,128)(2,1)} %all-gather.5.cloned.1.call-done), kind=kOutput, calls=%fused_computation.307 | convolution fusion | flops 1073741824 | bytes 5242880 | tf_op jit(solution)/shard_map/dot_general | solution.py:210
  346.8 1.4 fusion.106
  348.2 2.3 fusion.107
  350.5 2.3 fusion.108
  352.8 2.4 fusion.109
  355.1 2.2 convolution_add_fusion.1
  357.3 2.3 convolution_convert_fusion
  359.6 3.7 all-to-all-start.1
  363.3 3.0 fusion.12
  367.5 1.6 copy.455
  369.1 2.4 copy.456
  371.5 2.8 multiply_add_fusion
  374.3 3.4 all-to-all-done.1
  378.8 2.7 collective-permute-start.12
  382.2 1.3 mul.602
  383.5 2.5 mul.603
  387.2 2.9 fusion.88
  390.1 4.5 %collective-permute-done.12 = bf16[128,4096]{1,0:T(8,128)(2,1)} collective-permute-done((bf16[128,4096]{1,0:T(8,128)(2,1)}, bf16[128,4096]{1,0:T(8,128)(2,1)}, u32[]{:S(2)}, u32[]{:S(2)}) %collective-permute-start.12) | collective-permute-done | bytes 1048608 | tf_op jit(solution)/shard_map/ppermute | solution.py:29
  394.6 1.7 slice_bitcast_fusion.1
  396.2 2.3 copy.484
  (211 shorter events, 52.0 us)
Async XLA Ops:
  7.2 41.1 %all-gather.3.cloned.1.call-start = ((), (), s32[]{:S(2)}) async-start(), calls=%async_computation.4 | async-start | bytes 1179648 | tf_op jit(solution)/shard_map/all_gather | solution.py:90
  8.8 135.7 %reduce-scatter.3.cloned.1.call-start = ((), (), s32[]{:S(2)}) async-start(), calls=%async_computation.5 | async-start | bytes 4718592 | tf_op jit(solution)/shard_map/reduce_scatter | solution.py:95
  38.8 13.9 %copy-start.10 = (bf16[8,128,512]{2,1,0:T(8,128)(2,1)}, bf16[8,128,512]{2,1,0:T(8,128)(2,1)S(1)}, u32[]{:S(2)}) copy-start(bf16[8,128,512]{2,1,0:T(8,128)(2,1)S(1)} %all_to_all.24) | copy-start | bytes 3145732
  52.8 288.5 %all-gather.5.cloned.1.call-start = ((), (), s32[]{:S(2)}) async-start(), calls=%async_computation.6 | async-start | bytes 2359296 | tf_op jit(solution)/shard_map/all_gather | solution.py:208
  58.8 89.0 %copy-start.21 = (f32[128,64]{1,0:T(8,128)S(1)}, f32[128,64]{1,0:T(8,128)}, u32[]{:S(2)}) copy-start(f32[128,64]{1,0:T(8,128)} %copy-done.20) | copy-start | bytes 98308
  58.8 89.0 %copy-start.25 = (f32[128,64]{1,0:T(8,128)S(1)}, f32[128,64]{1,0:T(8,128)}, u32[]{:S(2)}) copy-start(f32[128,64]{1,0:T(8,128)} %copy-done.24) | copy-start | bytes 98308
  148.0 32.5 %copy-start.16 = (bf16[128,4,64]{2,0,1:T(8,128)(2,1)}, bf16[128,4,64]{2,0,1:T(8,128)(2,1)S(1)}, u32[]{:S(2)}) copy-start(bf16[128,4,64]{2,0,1:T(8,128)(2,1)S(1)} %get-tuple-element.17) | copy-start | bytes 196612
  148.9 26.8 %collective-permute-start = (bf16[2,128,4,128]{3,1,2,0:T(8,128)(2,1)}, bf16[2,128,4,128]{3,1,2,0:T(8,128)(2,1)}, u32[]{:S(2)}, u32[]{:S(2)}) collective-permute-start(bf16[2,128,4,128]{3,1,2,0:T(8,128)(2,1)} %pad_maximum_fusion.2), channel_id=1, source_target_pairs={{0,4},{4,8},{8,12},{12,16},{16,20},{20,24},{24,28},{28,32},{32,36}... | collective-permute-start | bytes 786440 | tf_op jit(solution)/shard_map/ppermute | solution.py:24
  152.8 27.7 %collective-permute-start.2 = (bf16[2,128,4,128]{3,1,2,0:T(8,128)(2,1)}, bf16[2,128,4,128]{3,1,2,0:T(8,128)(2,1)S(1)}, u32[]{:S(2)}, u32[]{:S(2)}) collective-permute-start(bf16[2,128,4,128]{3,1,2,0:T(8,128)(2,1)} %pad_maximum_fusion.2), channel_id=1, source_target_pairs={{0,12},{4,16},{8,20},{12,24},{16,28},{20,32},{24,36},{28,40},{32,4... | collective-permute-start | bytes 786440 | tf_op jit(solution)/shard_map/ppermute | solution.py:24
  158.5 22.4 %collective-permute-start.3 = (bf16[2,128,4,128]{3,1,2,0:T(8,128)(2,1)}, bf16[2,128,4,128]{3,1,2,0:T(8,128)(2,1)}, u32[]{:S(2)}, u32[]{:S(2)}) collective-permute-start(bf16[2,128,4,128]{3,1,2,0:T(8,128)(2,1)} %pad_maximum_fusion.2), channel_id=1, source_target_pairs={{0,16},{4,20},{8,24},{12,28},{16,32},{20,36},{24,40},{28,44},{32,4... | collective-permute-start | bytes 786440 | tf_op jit(solution)/shard_map/ppermute | solution.py:24
  161.3 26.4 %collective-permute-start.4 = (bf16[2,128,4,128]{3,1,2,0:T(8,128)(2,1)}, bf16[2,128,4,128]{3,1,2,0:T(8,128)(2,1)}, u32[]{:S(2)}, u32[]{:S(2)}) collective-permute-start(bf16[2,128,4,128]{3,1,2,0:T(8,128)(2,1)} %pad_maximum_fusion.2), channel_id=1, source_target_pairs={{0,20},{4,24},{8,28},{12,32},{16,36},{20,40},{24,44},{28,48},{32,5... | collective-permute-start | bytes 786440 | tf_op jit(solution)/shard_map/ppermute | solution.py:24
  167.5 33.0 %collective-permute-start.5 = (bf16[2,128,4,128]{3,1,2,0:T(8,128)(2,1)}, bf16[2,128,4,128]{3,1,2,0:T(8,128)(2,1)}, u32[]{:S(2)}, u32[]{:S(2)}) collective-permute-start(bf16[2,128,4,128]{3,1,2,0:T(8,128)(2,1)} %pad_maximum_fusion.2), channel_id=1, source_target_pairs={{0,24},{4,28},{8,32},{12,36},{16,40},{20,44},{24,48},{28,52},{32,5... | collective-permute-start | bytes 786440 | tf_op jit(solution)/shard_map/ppermute | solution.py:24
  174.5 30.5 %copy-start.30 = (bf16[128,4,128,1]{0,2,3,1:T(8,128)(2,1)}, bf16[128,4,128,1]{0,2,3,1:T(8,128)(2,1)S(1)}, u32[]{:S(2)}) copy-start(bf16[128,4,128,1]{0,2,3,1:T(8,128)(2,1)S(1)} %copy.342) | copy-start | bytes 393220
  175.7 26.1 %collective-permute-start.1 = (bf16[2,128,4,128]{3,1,2,0:T(8,128)(2,1)}, bf16[2,128,4,128]{3,1,2,0:T(8,128)(2,1)S(1)}, u32[]{:S(2)}, u32[]{:S(2)}) collective-permute-start(bf16[2,128,4,128]{3,1,2,0:T(8,128)(2,1)} %pad_maximum_fusion.2), channel_id=1, source_target_pairs={{0,8},{4,12},{8,16},{12,20},{16,24},{20,28},{24,32},{28,36},{32,40... | collective-permute-start | bytes 786440 | tf_op jit(solution)/shard_map/ppermute | solution.py:24
  180.5 35.7 %copy-start.34 = (bf16[2,128,4,128]{3,1,2,0:T(8,128)(2,1)}, bf16[2,128,4,128]{3,1,2,0:T(8,128)(2,1)S(1)}, u32[]{:S(2)}) copy-start(bf16[2,128,4,128]{3,1,2,0:T(8,128)(2,1)S(1)} %collective-permute-done.2) | copy-start | bytes 786436
  201.8 12.4 %copy-start.32 = (bf16[2,128,4,128]{3,1,2,0:T(8,128)(2,1)}, bf16[2,128,4,128]{3,1,2,0:T(8,128)(2,1)S(1)}, u32[]{:S(2)}) copy-start(bf16[2,128,4,128]{3,1,2,0:T(8,128)(2,1)S(1)} %collective-permute-done.1) | copy-start | bytes 786436
  212.6 2.3 copy-start.6
  212.9 13.5 %collective-permute-start.6 = (bf16[2,128,4,128]{3,1,2,0:T(8,128)(2,1)S(1)}, bf16[2,128,4,128]{3,1,2,0:T(8,128)(2,1)S(1)}, u32[]{:S(2)}, u32[]{:S(2)}) collective-permute-start(bf16[2,128,4,128]{3,1,2,0:T(8,128)(2,1)S(1)} %pad_maximum_fusion.3), channel_id=1, source_target_pairs={{4,0},{8,4},{12,8},{16,12},{20,16},{24,20},{28,24},{32,28},{36,32}... | collective-permute-start | bytes 786440 | tf_op jit(solution)/shard_map/ppermute | solution.py:24
  214.9 20.5 %collective-permute-start.7 = (bf16[2,128,4,128]{3,1,2,0:T(8,128)(2,1)S(1)}, bf16[2,128,4,128]{3,1,2,0:T(8,128)(2,1)S(1)}, u32[]{:S(2)}, u32[]{:S(2)}) collective-permute-start(bf16[2,128,4,128]{3,1,2,0:T(8,128)(2,1)S(1)} %pad_maximum_fusion.4), channel_id=1, source_target_pairs={{8,0},{12,4},{16,8},{20,12},{24,16},{28,20},{32,24},{36,28},{40,32... | collective-permute-start | bytes 786440 | tf_op jit(solution)/shard_map/ppermute | solution.py:24
  216.8 27.8 %collective-permute-start.8 = (bf16[2,128,4,128]{3,1,2,0:T(8,128)(2,1)S(1)}, bf16[2,128,4,128]{3,1,2,0:T(8,128)(2,1)S(1)}, u32[]{:S(2)}, u32[]{:S(2)}) collective-permute-start(bf16[2,128,4,128]{3,1,2,0:T(8,128)(2,1)S(1)} %pad_maximum_fusion.5), channel_id=1, source_target_pairs={{12,0},{16,4},{20,8},{24,12},{28,16},{32,20},{36,24},{40,28},{44,3... | collective-permute-start | bytes 786440 | tf_op jit(solution)/shard_map/ppermute | solution.py:24
  219.3 3.2 copy-start
  219.7 25.0 %collective-permute-start.9 = (bf16[2,128,4,128]{3,1,2,0:T(8,128)(2,1)S(1)}, bf16[2,128,4,128]{3,1,2,0:T(8,128)(2,1)S(1)}, u32[]{:S(2)}, u32[]{:S(2)}) collective-permute-start(bf16[2,128,4,128]{3,1,2,0:T(8,128)(2,1)S(1)} %pad_maximum_fusion.6), channel_id=1, source_target_pairs={{16,0},{20,4},{24,8},{28,12},{32,16},{36,20},{40,24},{44,28},{48,3... | collective-permute-start | bytes 786440 | tf_op jit(solution)/shard_map/ppermute | solution.py:24
  222.2 3.3 copy-start.2
  222.5 3.5 copy-start.31
  222.6 22.1 %collective-permute-start.10 = (bf16[2,128,4,128]{3,1,2,0:T(8,128)(2,1)S(1)}, bf16[2,128,4,128]{3,1,2,0:T(8,128)(2,1)S(1)}, u32[]{:S(2)}, u32[]{:S(2)}) collective-permute-start(bf16[2,128,4,128]{3,1,2,0:T(8,128)(2,1)S(1)} %pad_maximum_fusion.7), channel_id=1, source_target_pairs={{20,0},{24,4},{28,8},{32,12},{36,16},{40,20},{44,24},{48,28},{52,3... | collective-permute-start | bytes 786440 | tf_op jit(solution)/shard_map/ppermute | solution.py:24
  226.4 32.6 %collective-permute-start.11 = (bf16[2,128,4,128]{3,1,2,0:T(8,128)(2,1)S(1)}, bf16[2,128,4,128]{3,1,2,0:T(8,128)(2,1)S(1)}, u32[]{:S(2)}, u32[]{:S(2)}) collective-permute-start(bf16[2,128,4,128]{3,1,2,0:T(8,128)(2,1)S(1)} %pad_maximum_fusion.8), channel_id=1, source_target_pairs={{24,0},{28,4},{32,8},{36,12},{40,16},{44,20},{48,24},{52,28},{56,3... | collective-permute-start | bytes 786440 | tf_op jit(solution)/shard_map/ppermute | solution.py:24
  228.0 31.4 %copy-start.22 = (f32[128,64]{1,0:T(8,128)S(1)}, f32[128,64]{1,0:T(8,128)}, u32[]{:S(2)}) copy-start(f32[128,64]{1,0:T(8,128)} %copy-done.20) | copy-start | bytes 98308
  228.0 31.4 %copy-start.26 = (f32[128,64]{1,0:T(8,128)S(1)}, f32[128,64]{1,0:T(8,128)}, u32[]{:S(2)}) copy-start(f32[128,64]{1,0:T(8,128)} %copy-done.24) | copy-start | bytes 98308
  259.3 3.0 copy-start.29
  262.4 3.3 copy-start.38
  263.2 131.4 %reduce-scatter.5.cloned.1.call-start = ((), (), s32[]{:S(2)}) async-start(), calls=%async_computation.7 | async-start | bytes 2359296 | tf_op jit(solution)/shard_map/reduce_scatter | solution.py:209
  265.8 75.5 %copy-start.11 = (bf16[8,128,512]{2,1,0:T(8,128)(2,1)S(1)}, bf16[8,128,512]{2,1,0:T(8,128)(2,1)}, u32[]{:S(2)}) copy-start(bf16[8,128,512]{2,1,0:T(8,128)(2,1)} %copy-done.10) | copy-start | bytes 3145732
  345.5 2.7 copy-start.1
  346.8 3.7 copy-start.3
  348.2 4.5 %copy-start.5 = (bf16[4,4,128,128]{2,3,1,0:T(8,128)(2,1)S(1)}, bf16[4,4,128,128]{2,3,1,0:T(8,128)(2,1)}, u32[]{:S(2)}) copy-start(bf16[4,4,128,128]{2,3,1,0:T(8,128)(2,1)} %copy-done.4) | copy-start | bytes 1572868
  350.5 4.6 %copy-start.7 = (bf16[4,4,128,128]{2,3,1,0:T(8,128)(2,1)S(1)}, bf16[4,4,128,128]{2,3,1,0:T(8,128)(2,1)}, u32[]{:S(2)}) copy-start(bf16[4,4,128,128]{2,3,1,0:T(8,128)(2,1)} %copy-done.6) | copy-start | bytes 1572868
  352.8 4.6 %copy-start.19 = (bf16[1024,1024]{1,0:T(8,128)(2,1)S(1)}, bf16[1024,1024]{1,0:T(8,128)(2,1)}, u32[]{:S(2)}) copy-start(bf16[1024,1024]{1,0:T(8,128)(2,1)} %all-gather.5.cloned.1.call-done) | copy-start | bytes 6291460
  352.8 4.6 %copy-start.41 = (bf16[512,1024]{1,0:T(8,128)(2,1)S(1)}, bf16[512,1024]{1,0:T(8,128)(2,1)}, u32[]{:S(2)}) copy-start(bf16[512,1024]{1,0:T(8,128)(2,1)} %all-gather.3.cloned.1.call-done) | copy-start | bytes 3145732
  359.6 3.7 copy-start.9
  359.6 3.7 copy-start.33
  359.6 18.1 %all-to-all-start.1 = ((bf16[8,128,512]{2,1,0:T(8,128)(2,1)}), bf16[8,128,512]{2,1,0:T(8,128)(2,1)S(1)}, u32[]{:S(2)}, u32[]{:S(2)}) async-start(bf16[8,128,512]{2,1,0:T(8,128)(2,1)} %bitcast.629), calls=%async_computation.3 | async-start | bytes 2097152 | tf_op jit(solution)/shard_map/all_to_all | solution.py:220
  367.5 4.0 copy-start.23
  367.5 4.0 copy-start.27
  377.7 3.8 copy-start.14
  377.7 3.8 copy-start.15
  378.8 15.8 %collective-permute-start.12 = (bf16[128,4096]{1,0:T(8,128)(2,1)}, bf16[128,4096]{1,0:T(8,128)(2,1)}, u32[]{:S(2)}, u32[]{:S(2)}) collective-permute-start(bf16[128,4096]{1,0:T(8,128)(2,1)} %bitcast.226), channel_id=1, source_target_pairs={{0,3},{1,0},{2,1},{3,2},{4,7},{5,4},{6,5},{7,6},{8,11},{9,8},{10,9... | collective-permute-start | bytes 3145736 | tf_op jit(solution)/shard_map/ppermute | solution.py:29
  383.5 3.7 copy-start.12
  383.5 3.7 copy-start.13
  (12 other events, 17.4 us)
Sparse Core Ops, SparseCore 0:
  10.3 37.9 all-gather.2
  52.9 91.5 reduce-scatter.2
  263.3 77.9 all-gather.4
  345.6 38.6 reduce-scatter.4
